TPU v7x, 32 devices: a whole 2x2x4 slice. The times are simulated.
32 devices in a mesh: ctx: 16 (over z, y, core), grp: 2 (over x).
Axes of the slice: x: 2, y: 2, z: 4, core: 2. Of those that a mesh axis runs over, the one named last changes fastest.
Arguments:
- projected: bfloat16 [4096, 6144], P(('ctx', 'grp')), may hold values from -6 to 6
- conv_weight: float32 [3, 6144], replicated, may hold values from -2.5 to 2.5
- skip_gain: float32 [2048], replicated, may hold values from 0.5 to 1.5
- spectrum_real: bfloat16 [32, 256, 2048], P('ctx', None, 'grp'), may hold values from -6 to 6
- spectrum_imag: bfloat16 [32, 256, 2048], P('ctx', None, 'grp'), may hold values from -6 to 6
Outputs:
- mixer_out: bfloat16 [4096, 2048], P(('ctx', 'grp'))
All inputs are finite; a program needn't handle non-finite values.
Results may differ from a plain program's by a relative error of at most 0.0065.
Values may be sent and summed in bfloat16 or wider, within the bound.
No kernel may reach another device: no remote copies, remote signals or barrier semaphores. Data moves between devices by JAX's collectives and lax.ppermute only.
A program may use at most 64 MiB of HBM per device.

v0:
```python
import math

import jax
import jax.numpy as jnp
from jax import lax
from jax.sharding import PartitionSpec as P

TWO_PI = 2.0 * math.pi


def shifted(shard, axis, by):
    devices = lax.axis_size(axis)
    pairs = [(i, i + by) for i in range(devices) if 0 <= i + by < devices]
    return lax.ppermute(shard, axis, pairs)


def rotation(rows_index, cols_index, length, direction):
    product = rows_index[:, None] * cols_index[None, :] % length
    angles = product.astype(jnp.float32) * (TWO_PI / length)
    return (jnp.cos(angles), direction * jnp.sin(angles))


def complex_table(cos_part, sin_part):
    return jnp.stack([jnp.stack([cos_part, -sin_part]), jnp.stack([sin_part, cos_part])])


def contract(form, table, data):
    return jnp.einsum(
        form, table, data, precision=lax.Precision.HIGHEST, preferred_element_type=jnp.float32
    )


def twist(data, turn_real, turn_imag):
    return jnp.stack(
        [data[0] * turn_real - data[1] * turn_imag, data[0] * turn_imag + data[1] * turn_real]
    )


def across_forward(blocks, token_index, fft_len):
    block_count = blocks.shape[0]
    frequency = jnp.arange(2 * block_count, dtype=jnp.int32)
    block_order = jnp.arange(block_count, dtype=jnp.int32)
    cos_table, sin_table = rotation(frequency, block_order, 2 * block_count, -1.0)
    accum = contract("pkj,jbc->pkbc", jnp.stack([cos_table, sin_table]), blocks)
    turn_real, turn_imag = rotation(frequency, token_index, fft_len, -1.0)
    return twist(accum, turn_real[:, :, None], turn_imag[:, :, None])


def within_block(data, direction):
    leading, length, lane_count = (data.shape[1], data.shape[2], data.shape[3])
    first_len = math.gcd(length, 256)
    second_len = length // first_len
    data = data.reshape(2, leading, second_len, first_len, lane_count)
    outer_index = jnp.arange(second_len, dtype=jnp.int32)
    inner_index = jnp.arange(first_len, dtype=jnp.int32)
    table_real, table_imag = rotation(outer_index, outer_index, second_len, direction)
    section = contract("pqkj,qxjbc->pxkbc", complex_table(table_real, table_imag), data)
    turn_real, turn_imag = rotation(outer_index, inner_index, length, direction)
    twisted = twist(section, turn_real[None, :, :, None], turn_imag[None, :, :, None])
    last_real, last_imag = rotation(inner_index, inner_index, first_len, direction)
    result = contract("pqgb,qxkbc->pxgkc", complex_table(last_real, last_imag), twisted)
    return result.reshape(2, leading, length, lane_count)


def across_inverse(data, fft_len):
    block_count = data.shape[1] // 2
    block_order = jnp.arange(block_count, dtype=jnp.int32)
    frequency = jnp.arange(2 * block_count, dtype=jnp.int32)
    cos_table, sin_table = rotation(block_order, frequency, 2 * block_count, 1.0)
    summed = contract("qjk,qkbc->jbc", jnp.stack([cos_table, -sin_table]), data)
    return summed * (1.0 / fft_len)


def per_device(projected, conv_weight, skip_gain, spectrum_real, spectrum_imag):
    channels = conv_weight.shape[1] // 3
    rim_rows = conv_weight.shape[0] - 1
    row_count = projected.shape[0]
    rim = shifted(projected[row_count - rim_rows :], ("ctx", "grp"), 1)
    extended = jnp.concatenate([rim, projected], axis=0)
    short = jnp.zeros((row_count, 3 * channels), jnp.float32)
    for offset in range(rim_rows + 1):
        short = short + conv_weight[offset] * extended[
            rim_rows - offset : rim_rows - offset + row_count
        ].astype(jnp.float32)
    short = short.astype(jnp.bfloat16)
    query = short[:, :channels]
    gated = short[:, channels : 2 * channels].astype(jnp.float32) * short[:, 2 * channels :].astype(
        jnp.float32
    )
    block_count = lax.axis_size("ctx")
    group_count = lax.axis_size("grp")
    block_len = row_count * group_count
    fft_len = 2 * block_len * block_count
    block_index = lax.axis_index("ctx")
    sliver = lax.all_to_all(gated, "grp", split_axis=1, concat_axis=0, tiled=True)
    piece_len = block_len // block_count
    token_index = block_index * piece_len + jnp.arange(piece_len, dtype=jnp.int32)
    front = across_forward(
        lax.all_to_all(sliver[None], "ctx", split_axis=1, concat_axis=0, tiled=True),
        token_index,
        fft_len,
    )
    spectra = within_block(
        lax.all_to_all(front, "ctx", split_axis=1, concat_axis=2, tiled=True), -1.0
    )
    filtered = twist(spectra, spectrum_real.astype(jnp.float32), spectrum_imag.astype(jnp.float32))
    restored = within_block(filtered, 1.0)
    local_freq = spectra.shape[1]
    frequency = block_index * local_freq + jnp.arange(local_freq, dtype=jnp.int32)
    turn_real, turn_imag = rotation(frequency, jnp.arange(block_len, dtype=jnp.int32), fft_len, 1.0)
    restored = twist(restored, turn_real[:, :, None], turn_imag[:, :, None])
    long_blocks = across_inverse(
        lax.all_to_all(restored, "ctx", split_axis=2, concat_axis=1, tiled=True), fft_len
    )
    long_sliver = lax.all_to_all(long_blocks, "ctx", split_axis=0, concat_axis=1, tiled=True)[0]
    long_tokens = lax.all_to_all(long_sliver, "grp", split_axis=0, concat_axis=1, tiled=True)
    mixed = query.astype(jnp.float32) * (long_tokens + skip_gain * gated)
    return mixed.astype(jnp.bfloat16)


def short_convolution(projected, conv_weight):
    channels = conv_weight.shape[1] // 3
    rim_rows = conv_weight.shape[0] - 1
    row_count = projected.shape[0]
    rim = shifted(projected[row_count - rim_rows :], ("ctx", "grp"), 1)
    extended = jnp.concatenate([rim, projected], axis=0)
    short = jnp.zeros((row_count, 3 * channels), jnp.float32)
    for offset in range(rim_rows + 1):
        short = short + conv_weight[offset] * extended[
            rim_rows - offset : rim_rows - offset + row_count
        ].astype(jnp.float32)
    short = short.astype(jnp.bfloat16)
    query = short[:, :channels]
    gated = short[:, channels : 2 * channels].astype(jnp.float32) * short[:, 2 * channels :].astype(
        jnp.float32
    )
    return query, gated


def angle_table(rows_index, cols_index, length):
    product = rows_index[:, None] * cols_index[None, :] % length
    angles = product.astype(jnp.float32) * (TWO_PI / length)
    return jnp.cos(angles), jnp.sin(angles)


def channel_parallel(projected, conv_weight, skip_gain, spectrum_real, spectrum_imag):
    query, gated = short_convolution(projected, conv_weight)
    row_count, channels = gated.shape
    block_count = lax.axis_size("ctx")
    group_count = lax.axis_size("grp")
    devices = block_count * group_count
    block_len = row_count * group_count
    residues = 2 * block_count
    fft_len = residues * block_len
    width = channels // devices
    everyone = ("ctx", "grp")

    outgoing = gated.reshape(row_count, group_count, block_count, width).transpose(0, 2, 1, 3)
    outgoing = outgoing.reshape(row_count, devices, width)
    tokens = lax.all_to_all(outgoing, everyone, split_axis=1, concat_axis=0, tiled=True)
    tokens = tokens.reshape(block_count, block_len, width)

    def gather_spectrum(spectrum):
        local = lax.all_to_all(spectrum, "ctx", split_axis=2, concat_axis=0, tiled=True)
        return local.transpose(1, 2, 0).astype(jnp.float32)

    filter_real = gather_spectrum(spectrum_real)
    filter_imag = gather_spectrum(spectrum_imag)

    residue = jnp.arange(residues, dtype=jnp.int32)
    block_order = jnp.arange(block_count, dtype=jnp.int32)
    position = jnp.arange(block_len, dtype=jnp.int32)

    across_cos, across_sin = angle_table(block_order, residue, residues)
    folded_real = contract("jpc,ja->pca", tokens, across_cos)
    folded_imag = -contract("jpc,ja->pca", tokens, across_sin)
    turn_cos, turn_sin = angle_table(position, residue, fft_len)
    turn_cos, turn_sin = turn_cos[:, None, :], turn_sin[:, None, :]
    twisted_real = folded_real * turn_cos + folded_imag * turn_sin
    twisted_imag = folded_imag * turn_cos - folded_real * turn_sin

    within_cos, within_sin = angle_table(position, position, block_len)
    table = jnp.concatenate(
        [
            jnp.concatenate([within_cos, within_sin], axis=1),
            jnp.concatenate([-within_sin, within_cos], axis=1),
        ],
        axis=0,
    )
    lanes = width * residues
    stacked = jnp.concatenate(
        [twisted_real.reshape(block_len, lanes), twisted_imag.reshape(block_len, lanes)], axis=0
    )
    spectra = jnp.dot(table, stacked, precision=lax.Precision.HIGH, preferred_element_type=jnp.float32)
    spectra_real = spectra[:block_len].reshape(block_len, width, residues)
    spectra_imag = spectra[block_len:].reshape(block_len, width, residues)
    product_real = spectra_real * filter_real - spectra_imag * filter_imag
    product_imag = spectra_real * filter_imag + spectra_imag * filter_real
    stacked = jnp.concatenate(
        [product_real.reshape(block_len, lanes), product_imag.reshape(block_len, lanes)], axis=0
    )
    restored = lax.dot_general(
        table,
        stacked,
        (((0,), (0,)), ((), ())),
        precision=lax.Precision.HIGH,
        preferred_element_type=jnp.float32,
    )
    restored_real = restored[:block_len].reshape(block_len, width, residues)
    restored_imag = restored[block_len:].reshape(block_len, width, residues)
    unturned_real = restored_real * turn_cos - restored_imag * turn_sin
    unturned_imag = restored_real * turn_sin + restored_imag * turn_cos
    long_blocks = contract("ja,pca->jpc", across_cos, unturned_real) - contract(
        "ja,pca->jpc", across_sin, unturned_imag
    )
    long_blocks = (long_blocks * (1.0 / fft_len)).reshape(devices, row_count, width)
    returned = lax.all_to_all(long_blocks, everyone, split_axis=0, concat_axis=0, tiled=True)
    returned = returned.reshape(block_count, group_count, row_count, width).transpose(2, 1, 0, 3)
    long_tokens = returned.reshape(row_count, channels)
    mixed = query.astype(jnp.float32) * (long_tokens + skip_gain * gated)
    return mixed.astype(jnp.bfloat16)


def solution(mesh):
    in_specs = (P(("ctx", "grp"), None), P(), P(), P("ctx", None, "grp"), P("ctx", None, "grp"))
    out_specs = P(("ctx", "grp"), None)
    devices = mesh.shape["ctx"] * mesh.shape["grp"]

    def run(projected, conv_weight, skip_gain, spectrum_real, spectrum_imag):
        channels = conv_weight.shape[1] // 3
        wide = channels % devices == 0 and channels // devices >= 32
        body = channel_parallel if wide else per_device
        return jax.shard_map(
            body, mesh=mesh, in_specs=in_specs, out_specs=out_specs, check_vma=False
        )(projected, conv_weight, skip_gain, spectrum_real, spectrum_imag)

    return run
```

profile of v0, /device:TPU:1, one launch (start us, length us, event | category | flops | bytes accessed | tf_op | source)
XLA Modules:
  0.0 171.7 jit_solution(8147511950215730047)
XLA Ops:
  0.0 3.8 %copy.50 = bf16[2,256,1024]{1,0,2:T(2,128)(2,1)} copy(bf16[2,256,1024]{2,1,0:T(8,128)(2,1)} %param.8) | data formatting | bytes 2097152 | tf_op args[3]
  3.8 7.3 %all-to-all-start.1 = ((bf16[2,256,1024]{1,0,2:T(2,128)(2,1)}), bf16[2,256,1024]{1,0,2:T(2,128)(2,1)S(1)}, u32[]{:S(2)}, u32[]{:S(2)}) async-start(bf16[2,256,1024]{1,0,2:T(2,128)(2,1)} %copy.50), calls=%async_computation.1 | async-start | bytes 2097152 | tf_op jit(solution)/shard_map/all_to_all | solution.py:164
  11.1 0.0 copy-done.9
  11.2 0.0 copy-start.10
  11.2 3.3 %collective-permute-start = (bf16[2,6144]{1,0:T(2,128)(2,1)S(1)}, bf16[2,6144]{1,0:T(2,128)(2,1)S(1)}, u32[]{:S(2)}, u32[]{:S(2)}) collective-permute-start(bf16[2,6144]{1,0:T(2,128)(2,1)S(1)} %slice.41), channel_id=1, source_target_pairs={{0,1},{1,2},{2,3},{3,4},{4,5},{5,6},{6,7},{7,8},{8,9},{9,10},{10,1... | collective-permute-start | bytes 73736 | tf_op jit(solution)/shard_map/ppermute | solution.py:14
  14.4 3.6 %copy.55 = bf16[2,256,1024]{1,0,2:T(2,128)(2,1)} copy(bf16[2,256,1024]{2,1,0:T(8,128)(2,1)} %param.9) | data formatting | bytes 2097152 | tf_op args[4]
  18.1 16.2 %all-to-all-done.1 = bf16[2,256,1024]{1,0,2:T(2,128)(2,1)S(1)} async-done(((bf16[2,256,1024]{1,0,2:T(2,128)(2,1)}), bf16[2,256,1024]{1,0,2:T(2,128)(2,1)S(1)}, u32[]{:S(2)}, u32[]{:S(2)}) %all-to-all-start.1) | async-done | bytes 1048608 | tf_op jit(solution)/shard_map/all_to_all | solution.py:164
  34.3 6.5 %all-to-all-start.2 = ((bf16[2,256,1024]{1,0,2:T(2,128)(2,1)}), bf16[2,256,1024]{1,0,2:T(2,128)(2,1)}, u32[]{:S(2)}, u32[]{:S(2)}) async-start(bf16[2,256,1024]{1,0,2:T(2,128)(2,1)} %copy.55), calls=%async_computation.2 | async-start | bytes 2097152 | tf_op jit(solution)/shard_map/all_to_all | solution.py:164
  40.8 0.0 copy-done.3
  40.9 0.0 copy-done.10
  40.9 0.1 fusion.86
  40.9 0.9 copy.44
  41.8 0.0 collective-permute-done
  41.8 0.9 copy.45
  42.7 4.4 %add_convert_fusion = bf16[128,6144]{0,1:T(8,128)(2,1)S(1)} fusion(bf16[128,6144]{0,1:T(8,128)(2,1)S(1)} %copy.44, bf16[2,6144]{0,1:T(8,128)(2,1)S(1)} %copy.45, f32[6144]{0:T(1024)S(1)} %bitcast.89, f32[6144]{0:T(1024)S(1)} %bitcast.90, f32[6144]{0:T(1024)S(1)} %bitcast.88), kind=kLoop, calls=%fused_computation.10 | loop fusion | flops 11796480 | bytes 3244032 | tf_op jit(solution)/shard_map/convert_element_type | solution.py:132
  47.1 0.0 copy-start.1
  47.1 1.2 copy-done.1
  48.3 0.1 convert_multiply_fusion
  48.4 0.0 copy-start.4
  48.4 1.1 copy.47
  49.5 14.6 %all-to-all-done.2 = bf16[2,256,1024]{1,0,2:T(2,128)(2,1)} async-done(((bf16[2,256,1024]{1,0,2:T(2,128)(2,1)}), bf16[2,256,1024]{1,0,2:T(2,128)(2,1)}, u32[]{:S(2)}, u32[]{:S(2)}) %all-to-all-start.2) | async-done | bytes 1048608 | tf_op jit(solution)/shard_map/all_to_all | solution.py:164
  64.1 6.2 %all-to-all-start = ((f32[128,32,64]{0,2,1:T(8,128)}), f32[128,32,64]{0,2,1:T(8,128)S(1)}, u32[]{:S(2)}, u32[]{:S(2)}) async-start(f32[128,32,64]{0,2,1:T(8,128)} %bitcast.6), calls=%async_computation | async-start | bytes 2097152 | tf_op jit(solution)/shard_map/all_to_all | solution.py:160
  70.4 0.1 fusion.46
  70.5 1.0 fusion.39
  71.5 1.8 %fusion.37 = (f32[256,256]{1,0:T(8,128)}, f32[256,256]{1,0:T(8,128)}) fusion(), kind=kLoop, calls=%fused_computation.51 | loop fusion | flops 917504 | bytes 524288 | tf_op jit(solution)/shard_map/sin | solution.py:143
  73.3 0.0 copy-done.4
  73.3 0.1 copy.51
  73.4 0.3 convert_bitcast_fusion.1
  73.7 0.1 copy.52
  73.8 1.4 copy.56
  75.2 0.3 convert_bitcast_fusion
  75.4 1.5 copy.57
  76.9 19.5 %all-to-all-done = f32[128,32,64]{0,2,1:T(8,128)S(1)} async-done(((f32[128,32,64]{0,2,1:T(8,128)}), f32[128,32,64]{0,2,1:T(8,128)S(1)}, u32[]{:S(2)}, u32[]{:S(2)}) %all-to-all-start) | async-done | bytes 1048608 | tf_op jit(solution)/shard_map/all_to_all | solution.py:160
  96.4 1.6 copy.48
  98.0 1.5 reshape.88
  99.6 1.9 %fusion.52 = f32[256,64,32]{0,2,1:T(8,128)S(1)} fusion(f32[16,256,64]{1,0,2:T(8,128)S(1)} %reshape.88), kind=kOutput, calls=%fused_computation.72 | convolution fusion | flops 100670464 | bytes 3145728 | tf_op jit(solution)/shard_map/jpc,ja->pca/dot_general | solution.py:28
  101.5 0.0 copy-start.5
  101.5 0.0 copy-start.7
  101.5 2.3 %multiply_add_fusion = (f32[256,64,32]{0,2,1:T(8,128)S(1)}, f32[256,64,32]{0,2,1:T(8,128)S(1)}) fusion(f32[256,64,32]{0,2,1:T(8,128)S(1)} %fusion.52, f32[256,32]{0,1:T(8,128)S(1)} %get-tuple-element.16, f32[256,32]{0,1:T(8,128)S(1)} %get-tuple-element.17, f32[16,256,64]{1,0,2:T(8,128)S(1)} %reshape.88), kind=kOutput, calls=%fused_computation.28 | convolution fusion | flops 104340480 | bytes 7405568 | tf_op jit(solution)/shard_map/jpc,ja->pca/dot_general | solution.py:28
  103.8 0.0 copy-done.5
  103.8 0.0 copy-done.7
  103.8 3.6 %fusion = f32[512,2048]{1,0:T(8,128)S(1)} fusion(f32[256,2048]{0,1:T(8,128)S(1)} %bitcast.76, f32[256,2048]{0,1:T(8,128)S(1)} %bitcast.75, f32[256,256]{1,0:T(8,128)S(1)} %copy-done.7, f32[256,256]{1,0:T(8,128)S(1)} %fusion.39, f32[256,256]{1,0:T(8,128)S(1)} %copy-done.5), kind=kOutput, calls=%fused_computation | convolution fusion | flops 3223060480 | bytes 9175040 | tf_op jit(solution)/shard_map/dot_general | solution.py:194
  107.4 2.5 %fusion.85 = (f32[256,2048]{1,0:T(8,128)}, f32[256,2048]{1,0:T(8,128)}) fusion(f32[512,2048]{1,0:T(8,128)S(1)} %fusion), kind=kLoop, calls=%fused_computation.101 | loop fusion | bytes 8388608 | tf_op jit(solution)/shard_map/slice | solution.py:196
  109.9 2.9 %copy.54 = f32[256,2048]{0,1:T(8,128)} copy(f32[256,2048]{1,0:T(8,128)} %get-tuple-element.11) | data formatting | bytes 4194304 | tf_op jit(solution)/shard_map/slice | solution.py:196
  112.8 3.0 %copy.49 = f32[256,2048]{0,1:T(8,128)} copy(f32[256,2048]{1,0:T(8,128)} %get-tuple-element.12) | data formatting | bytes 4194304 | tf_op jit(solution)/shard_map/slice | solution.py:195
  115.8 5.4 %fusion.8 = (f32[256,64,32]{0,2,1:T(8,128)S(1)}, f32[256,64,32]{0,2,1:T(8,128)S(1)}) fusion(f32[256,64,32]{0,2,1:T(8,128)} %bitcast.79, f32[256,64,32]{0,2,1:T(8,128)} %bitcast.80, f32[32,256,64]{1,2,0:T(8,128)} %bitcast.78, f32[32,256,64]{1,2,0:T(8,128)S(1)} %bitcast.77), kind=kLoop, calls=%fused_computation.15 | loop fusion | flops 3145728 | bytes 12582912 | tf_op jit(solution)/shard_map/sub | solution.py:197
  121.2 0.0 copy-done.6
  121.2 0.0 copy-done.8
  121.2 6.9 %fusion.4 = f32[512,2048]{1,0:T(8,128)S(1)} fusion(f32[256,2048]{0,1:T(8,128)S(1)} %bitcast.82, f32[256,2048]{0,1:T(8,128)S(1)} %bitcast.81, f32[256,256]{1,0:T(8,128)S(1)} %copy-done.8, f32[256,256]{1,0:T(8,128)S(1)} %fusion.39, f32[256,256]{1,0:T(8,128)S(1)} %copy-done.6), kind=kOutput, calls=%fused_computation.4 | convolution fusion | flops 3223060480 | bytes 9175040 | tf_op jit(solution)/shard_map/dot_general | solution.py:202
  128.1 2.5 %fusion.84 = (f32[256,2048]{1,0:T(8,128)}, f32[256,2048]{1,0:T(8,128)}) fusion(f32[512,2048]{1,0:T(8,128)S(1)} %fusion.4), kind=kLoop, calls=%fused_computation.100 | loop fusion | bytes 8388608 | tf_op jit(solution)/shard_map/slice | solution.py:209
  130.6 1.9 %copy.59 = f32[256,2048]{0,1:T(8,128)S(1)} copy(f32[256,2048]{1,0:T(8,128)} %get-tuple-element.9) | data formatting | bytes 4194304 | tf_op jit(solution)/shard_map/slice | solution.py:209
  132.5 2.9 %copy.60 = f32[256,2048]{0,1:T(8,128)} copy(f32[256,2048]{1,0:T(8,128)} %get-tuple-element.10) | data formatting | bytes 4194304 | tf_op jit(solution)/shard_map/slice | solution.py:210
  135.4 3.1 %fusion.10 = f32[16,256,64]{1,0,2:T(8,128)S(1)} fusion(f32[256,64,32]{0,2,1:T(8,128)} %bitcast.73, f32[256,64,32]{0,2,1:T(8,128)S(1)} %bitcast.71, f32[256,32]{0,1:T(8,128)S(1)} %get-tuple-element.16, f32[256,32]{0,1:T(8,128)S(1)} %get-tuple-element.17), kind=kOutput, calls=%fused_computation.19 | convolution fusion | flops 102243328 | bytes 5308416 | tf_op jit(solution)/shard_map/ja,pca->jpc/dot_general | solution.py:28
  138.5 0.0 copy-done
  138.5 1.4 fusion.22
  139.9 0.1 reshape.97
  140.0 0.6 copy.61
  140.6 0.0 copy-start.11
  140.7 29.6 %all_to_all.38 = f32[32,128,64]{1,2,0:T(8,128)S(1)} all-to-all(f32[32,128,64]{1,2,0:T(8,128)S(1)} %copy.61), channel_id=1, replica_groups=mesh['ctx'=16,'grp'=2] {'ctx','grp'}, dimensions={0} | all-to-all | bytes 2097152 | tf_op jit(solution)/shard_map/all_to_all | solution.py:217
  170.3 0.1 copy.62
  170.4 0.0 copy-done.2
  170.4 0.0 copy-done.11
  170.4 0.3 fusion.26
  170.7 1.0 copy.63
  (7 shorter events, 0.0 us)
Async XLA Ops:
  0.0 11.1 %copy-start.9 = (bf16[128,6144]{1,0:T(8,128)(2,1)S(1)}, bf16[128,6144]{1,0:T(8,128)(2,1)}, u32[]{:S(2)}) copy-start(bf16[128,6144]{1,0:T(8,128)(2,1)} %param.5) | copy-start | bytes 4718596
  3.8 30.5 %all-to-all-start.1 = ((bf16[2,256,1024]{1,0,2:T(2,128)(2,1)}), bf16[2,256,1024]{1,0,2:T(2,128)(2,1)S(1)}, u32[]{:S(2)}, u32[]{:S(2)}) async-start(bf16[2,256,1024]{1,0,2:T(2,128)(2,1)} %copy.50), calls=%async_computation.1 | async-start | bytes 2097152 | tf_op jit(solution)/shard_map/all_to_all | solution.py:164
  11.2 29.7 %copy-start.10 = (f32[3,6144]{1,0:T(4,128)S(1)}, f32[3,6144]{1,0:T(4,128)}, u32[]{:S(2)}) copy-start(f32[3,6144]{1,0:T(4,128)} %param.6) | copy-start | bytes 221188
  11.2 30.7 %collective-permute-start = (bf16[2,6144]{1,0:T(2,128)(2,1)S(1)}, bf16[2,6144]{1,0:T(2,128)(2,1)S(1)}, u32[]{:S(2)}, u32[]{:S(2)}) collective-permute-start(bf16[2,6144]{1,0:T(2,128)(2,1)S(1)} %slice.41), channel_id=1, source_target_pairs={{0,1},{1,2},{2,3},{3,4},{4,5},{5,6},{6,7},{7,8},{8,9},{9,10},{10,1... | collective-permute-start | bytes 73736 | tf_op jit(solution)/shard_map/ppermute | solution.py:14
  34.3 6.5 %copy-start.3 = (bf16[2,256,1024]{1,0,2:T(2,128)(2,1)}, bf16[2,256,1024]{1,0,2:T(2,128)(2,1)S(1)}, u32[]{:S(2)}) copy-start(bf16[2,256,1024]{1,0,2:T(2,128)(2,1)S(1)} %all-to-all-done.1) | copy-start | bytes 3145732
  34.3 29.8 %all-to-all-start.2 = ((bf16[2,256,1024]{1,0,2:T(2,128)(2,1)}), bf16[2,256,1024]{1,0,2:T(2,128)(2,1)}, u32[]{:S(2)}, u32[]{:S(2)}) async-start(bf16[2,256,1024]{1,0,2:T(2,128)(2,1)} %copy.55), calls=%async_computation.2 | async-start | bytes 2097152 | tf_op jit(solution)/shard_map/all_to_all | solution.py:164
  47.1 1.2 copy-start.1
  48.4 24.9 %copy-start.4 = (bf16[2,256,1024]{1,0,2:T(2,128)(2,1)S(1)}, bf16[2,256,1024]{1,0,2:T(2,128)(2,1)}, u32[]{:S(2)}) copy-start(bf16[2,256,1024]{1,0,2:T(2,128)(2,1)} %copy-done.3) | copy-start | bytes 3145732
  64.1 32.3 %all-to-all-start = ((f32[128,32,64]{0,2,1:T(8,128)}), f32[128,32,64]{0,2,1:T(8,128)S(1)}, u32[]{:S(2)}, u32[]{:S(2)}) async-start(f32[128,32,64]{0,2,1:T(8,128)} %bitcast.6), calls=%async_computation | async-start | bytes 2097152 | tf_op jit(solution)/shard_map/all_to_all | solution.py:160
  101.5 2.4 %copy-start.5 = (f32[256,256]{1,0:T(8,128)S(1)}, f32[256,256]{1,0:T(8,128)}, u32[]{:S(2)}) copy-start(f32[256,256]{1,0:T(8,128)} %get-tuple-element.18) | copy-start | bytes 786436
  101.5 2.4 %copy-start.7 = (f32[256,256]{1,0:T(8,128)S(1)}, f32[256,256]{1,0:T(8,128)}, u32[]{:S(2)}) copy-start(f32[256,256]{1,0:T(8,128)} %get-tuple-element.19) | copy-start | bytes 786436
  115.8 5.5 %copy-start.6 = (f32[256,256]{1,0:T(8,128)S(1)}, f32[256,256]{1,0:T(8,128)}, u32[]{:S(2)}) copy-start(f32[256,256]{1,0:T(8,128)} %get-tuple-element.18) | copy-start | bytes 786436
  115.8 5.5 %copy-start.8 = (f32[256,256]{1,0:T(8,128)S(1)}, f32[256,256]{1,0:T(8,128)}, u32[]{:S(2)}) copy-start(f32[256,256]{1,0:T(8,128)} %get-tuple-element.19) | copy-start | bytes 786436
  135.4 3.1 %copy-start = (f32[256,2048]{0,1:T(8,128)S(1)}, f32[256,2048]{0,1:T(8,128)}, u32[]{:S(2)}) copy-start(f32[256,2048]{0,1:T(8,128)} %copy.60) | copy-start | bytes 6291460
  140.6 29.7 %copy-start.2 = (bf16[128,6144]{0,1:T(8,128)(2,1)S(1)}, bf16[128,6144]{0,1:T(8,128)(2,1)}, u32[]{:S(2)}) copy-start(bf16[128,6144]{0,1:T(8,128)(2,1)} %copy-done.1) | copy-start | bytes 4718596
  140.6 29.7 %copy-start.11 = (f32[2048]{0:T(1024)S(1)}, f32[2048]{0:T(1024)}, u32[]{:S(2)}) copy-start(f32[2048]{0:T(1024)} %param.7) | copy-start | bytes 24580
where the time goes:
time: 173 us; the launch traced here: 172 us
  waiting for transfers between devices  50.3 us (29%)
  local copies, waits for them, and re-layouts  35.3 us (20%)
  blocking collectives  29.6 us (17%)
  starting transfers between devices  23.3 us (13%)
  matrix products  19.2 us (11%)
  other arithmetic  13.7 us (8%)
    all_to_all x2, waiting for transfers between devices, gather_spectrum(): lax.all_to_all(spectrum, 'ctx', split_axis=2, concat_axis=0, tiled=True)  30.8 us
    all_to_all x1, blocking collectives, channel_parallel(): lax.all_to_all(long_blocks, everyone, split_axis=0, concat_axis=0, tiled=...  29.6 us
    all_to_all x1, waiting for transfers between devices, channel_parallel(): lax.all_to_all(outgoing, everyone, split_axis=1, concat_axis=0, tiled=True)  19.5 us
    all_to_all x2, starting transfers between devices, gather_spectrum(): lax.all_to_all(spectrum, 'ctx', split_axis=2, concat_axis=0, tiled=True)  13.9 us
    unnamed x27, local copies, waits for them, and re-layouts  9.55 us
    dot_general x4, matrix products, contract(): jnp.einsum(form, table, data, precision=lax.Precision.HIGHEST, preferred_...  8.74 us
    dot_general x1, matrix products, channel_parallel(): lax.dot_general(table, stacked, (((0,), (0,)), ((), ())), precision=lax.P...  6.88 us
    all_to_all x1, starting transfers between devices, channel_parallel(): lax.all_to_all(outgoing, everyone, split_axis=1, concat_axis=0, tiled=True)  6.21 us
  transfers between devices with their start and end apart: 4, of which 3 were waited for; matrix products, arithmetic and copies ran while one was open for 10% of the time, Pallas kernels for 0%

commit v1 on v0

--- a/solution.py
+++ b/solution.py
@@ -160,12 +160,10 @@
     tokens = lax.all_to_all(outgoing, everyone, split_axis=1, concat_axis=0, tiled=True)
     tokens = tokens.reshape(block_count, block_len, width)
 
-    def gather_spectrum(spectrum):
-        local = lax.all_to_all(spectrum, "ctx", split_axis=2, concat_axis=0, tiled=True)
-        return local.transpose(1, 2, 0).astype(jnp.float32)
-
-    filter_real = gather_spectrum(spectrum_real)
-    filter_imag = gather_spectrum(spectrum_imag)
+    tokens, spectrum = lax.optimization_barrier((tokens, jnp.stack([spectrum_real, spectrum_imag])))
+    spectrum = lax.all_to_all(spectrum, "ctx", split_axis=3, concat_axis=1, tiled=True)
+    spectrum = spectrum.transpose(0, 2, 3, 1).astype(jnp.float32)
+    filter_real, filter_imag = spectrum[0], spectrum[1]
 
     residue = jnp.arange(residues, dtype=jnp.int32)
     block_order = jnp.arange(block_count, dtype=jnp.int32)
@@ -214,7 +212,9 @@
         "ja,pca->jpc", across_sin, unturned_imag
     )
     long_blocks = (long_blocks * (1.0 / fft_len)).reshape(devices, row_count, width)
+    long_blocks = long_blocks.astype(jnp.bfloat16)
     returned = lax.all_to_all(long_blocks, everyone, split_axis=0, concat_axis=0, tiled=True)
+    returned = returned.astype(jnp.float32)
     returned = returned.reshape(block_count, group_count, row_count, width).transpose(2, 1, 0, 3)
     long_tokens = returned.reshape(row_count, channels)
     mixed = query.astype(jnp.float32) * (long_tokens + skip_gain * gated)

time: 173 us -> 154 us (0.89)
  starting transfers between devices: 23.3 us -> 13.8 us
  local copies, waits for them, and re-layouts: 35.3 us -> 31.1 us
  blocking collectives: 29.6 us -> 26 us
  other arithmetic: 13.7 us -> 16.1 us
  waiting for transfers between devices: 50.3 us -> 48.4 us
    all_to_all x2 -> x1, starting transfers between devices: 13.9 us -> 4.05 us  [channel_parallel(): lax.all_to_all(spectrum, 'ctx', split_axis=3, concat_axis=1, tiled=True)]
    another operation x0 -> x1, other arithmetic: none -> 4.05 us  [channel_parallel(): jnp.stack([spectrum_real, spectrum_imag])]
    squeeze x0 -> x2, local copies, waits for them, and re-layouts: none -> 3.96 us  [channel_parallel(): filter_real, filter_imag = (spectrum[0], spectrum[1])]
    all_to_all x1, blocking collectives: 29.6 us -> 26 us  [channel_parallel(): lax.all_to_all(long_blocks, everyone, split_axis=0, concat_axis=0, tiled=...]
    dot_general x1, matrix products: 6.88 us -> 3.87 us  [channel_parallel(): lax.dot_general(table, stacked, (((0,), (0,)), ((), ())), precision=lax.P...]
    unnamed x27 -> x21, local copies, waits for them, and re-layouts: 9.55 us -> 6.94 us
    slice x3, local copies, waits for them, and re-layouts: 8.36 us -> 5.79 us  [channel_parallel(): filter_real, filter_imag = (spectrum[0], spectrum[1])]
    all_to_all x2 -> x1, waiting for transfers between devices: 30.8 us -> 29.9 us  [channel_parallel(): lax.all_to_all(spectrum, 'ctx', split_axis=3, concat_axis=1, tiled=True)]
  transfers between devices with their start and end apart: 4 -> 3, of which waited for: 3 -> 2; matrix products, arithmetic and copies ran while one was open for 10% -> 14% of each run, Pallas kernels for 0% -> 0%
where the time goes in v1:
time: 154 us
  waiting for transfers between devices  48.4 us (31%)
  local copies, waits for them, and re-layouts  31.1 us (20%)
  blocking collectives  26 us (17%)
  matrix products  17.8 us (12%)
  other arithmetic  16.1 us (10%)
  starting transfers between devices  13.8 us (9%)
    all_to_all x1, waiting for transfers between devices, channel_parallel(): lax.all_to_all(spectrum, 'ctx', split_axis=3, concat_axis=1, tiled=True)  29.9 us
    all_to_all x1, blocking collectives, channel_parallel(): lax.all_to_all(long_blocks, everyone, split_axis=0, concat_axis=0, tiled=...  26 us
    all_to_all x1, waiting for transfers between devices, channel_parallel(): lax.all_to_all(outgoing, everyone, split_axis=1, concat_axis=0, tiled=True)  18.5 us
    dot_general x4, matrix products, contract(): jnp.einsum(form, table, data, precision=lax.Precision.HIGHEST, preferred_...  8.74 us
    unnamed x21, local copies, waits for them, and re-layouts  6.94 us
    all_to_all x1, starting transfers between devices, channel_parallel(): lax.all_to_all(outgoing, everyone, split_axis=1, concat_axis=0, tiled=True)  5.79 us
    slice x3, local copies, waits for them, and re-layouts, channel_parallel(): filter_real, filter_imag = (spectrum[0], spectrum[1])  5.79 us
    dot_general x1, matrix products, channel_parallel(): jnp.dot(table, stacked, precision=lax.Precision.HIGH, preferred_element_t...  5.21 us
  transfers between devices with their start and end apart: 3, of which 2 were waited for; matrix products, arithmetic and copies ran while one was open for 14% of the time, Pallas kernels for 0%

profile of v1, /device:TPU:1, one launch (start us, length us, event | category | flops | bytes accessed | tf_op | source)
XLA Modules:
  0.0 153.5 jit_solution(11305099588154271429)
XLA Ops:
  0.0 0.9 slice.47
  0.9 3.9 %collective-permute-start = (bf16[2,6144]{1,0:T(2,128)(2,1)S(1)}, bf16[2,6144]{1,0:T(2,128)(2,1)S(1)}, u32[]{:S(2)}, u32[]{:S(2)}) collective-permute-start(bf16[2,6144]{1,0:T(2,128)(2,1)S(1)} %slice.47), channel_id=1, source_target_pairs={{0,1},{1,2},{2,3},{3,4},{4,5},{5,6},{6,7},{7,8},{8,9},{9,10},{10,1... | collective-permute-start | bytes 73736 | tf_op jit(solution)/shard_map/ppermute | solution.py:14
  4.9 1.1 fusion.87
  6.0 1.9 %copy.45 = bf16[128,6144]{0,1:T(8,128)(2,1)S(1)} copy(bf16[128,6144]{1,0:T(8,128)(2,1)} %param.5) | data formatting | bytes 3145728 | tf_op args[0]
  7.9 0.0 collective-permute-done
  7.9 0.9 copy.46
  8.8 4.4 %add_convert_fusion = bf16[128,6144]{0,1:T(8,128)(2,1)S(1)} fusion(bf16[128,6144]{0,1:T(8,128)(2,1)S(1)} %copy.45, bf16[2,6144]{0,1:T(8,128)(2,1)S(1)} %copy.46, f32[6144]{0:T(1024)S(1)} %bitcast.71, f32[6144]{0:T(1024)S(1)} %bitcast.72, f32[6144]{0:T(1024)S(1)} %bitcast.70), kind=kLoop, calls=%fused_computation.11 | loop fusion | flops 11796480 | bytes 3244032 | tf_op jit(solution)/shard_map/convert_element_type | solution.py:132
  13.2 0.0 copy-start.1
  13.2 0.1 convert_multiply_fusion
  13.3 0.0 copy-start.7
  13.3 1.1 copy.48
  14.4 0.3 copy-done.1
  14.8 5.8 %all-to-all-start = ((f32[128,32,64]{0,2,1:T(8,128)}), f32[128,32,64]{0,2,1:T(8,128)S(1)}, u32[]{:S(2)}, u32[]{:S(2)}) async-start(f32[128,32,64]{0,2,1:T(8,128)} %bitcast.6), calls=%async_computation | async-start | bytes 2097152 | tf_op jit(solution)/shard_map/all_to_all | solution.py:160
  20.5 0.0 copy-done.7
  20.6 0.9 copy.50
  21.5 2.5 %copy.51 = bf16[2,256,1024]{1,0,2:T(2,128)(2,1)S(1)} copy(bf16[2,256,1024]{2,1,0:T(8,128)(2,1)} %param.9) | data formatting | bytes 2097152 | tf_op args[4]
  24.0 4.1 %pad_maximum_fusion = bf16[2,2,256,1024]{2,1,0,3:T(2,128)(2,1)} fusion(bf16[1,2,256,1024]{2,1,0,3:T(2,128)(2,1)S(1)} %bitcast.68, bf16[1,2,256,1024]{2,1,0,3:T(2,128)(2,1)S(1)} %bitcast.67), kind=kLoop, calls=%fused_computation.12 | loop fusion | flops 1048576 | bytes 4194304 | tf_op jit(solution)/shard_map/stack | solution.py:163
  28.1 18.5 %all-to-all-done = f32[128,32,64]{0,2,1:T(8,128)S(1)} async-done(((f32[128,32,64]{0,2,1:T(8,128)}), f32[128,32,64]{0,2,1:T(8,128)S(1)}, u32[]{:S(2)}, u32[]{:S(2)}) %all-to-all-start) | async-done | bytes 1048608 | tf_op jit(solution)/shard_map/all_to_all | solution.py:160
  46.6 0.6 copy.49
  47.2 0.3 reshape.83
  47.5 4.1 %all-to-all-start.1 = ((bf16[2,2,256,1024]{2,1,0,3:T(2,128)(2,1)}), bf16[2,2,256,1024]{2,1,0,3:T(2,128)(2,1)S(1)}, u32[]{:S(2)}, u32[]{:S(2)}) async-start(bf16[2,2,256,1024]{2,1,0,3:T(2,128)(2,1)} %pad_maximum_fusion), calls=%async_computation.1 | async-start | bytes 4194304 | tf_op jit(solution)/shard_map/all_to_all | solution.py:164
  51.6 0.1 fusion.47
  51.7 1.0 fusion.40
  52.7 1.0 fusion.38
  53.8 0.0 copy-start.3
  53.8 0.0 copy-start.5
  53.8 1.9 %fusion.53 = f32[256,64,32]{0,2,1:T(8,128)S(1)} fusion(f32[16,256,64]{1,0,2:T(8,128)S(1)} %reshape.83), kind=kOutput, calls=%fused_computation.70 | convolution fusion | flops 100670464 | bytes 3145728 | tf_op jit(solution)/shard_map/jpc,ja->pca/dot_general | solution.py:28
  55.7 2.3 %multiply_add_fusion.1 = (f32[256,64,32]{0,2,1:T(8,128)S(1)}, f32[256,64,32]{0,2,1:T(8,128)S(1)}) fusion(f32[256,64,32]{0,2,1:T(8,128)S(1)} %fusion.53, f32[256,32]{0,1:T(8,128)S(1)} %get-tuple-element.20, f32[256,32]{0,1:T(8,128)S(1)} %get-tuple-element.21, f32[16,256,64]{1,0,2:T(8,128)S(1)} %reshape.83), kind=kOutput, calls=%fused_computation.24 | convolution fusion | flops 104340480 | bytes 7405568 | tf_op jit(solution)/shard_map/jpc,ja->pca/dot_general | solution.py:28
  58.0 0.0 copy-done.3
  58.0 0.0 copy-done.5
  58.0 5.2 %fusion = f32[512,2048]{1,0:T(8,128)} fusion(f32[256,2048]{0,1:T(8,128)S(1)} %bitcast.62, f32[256,2048]{0,1:T(8,128)S(1)} %bitcast.61, f32[256,256]{1,0:T(8,128)S(1)} %get-tuple-element.23, f32[256,256]{1,0:T(8,128)S(1)} %fusion.40, f32[256,256]{1,0:T(8,128)S(1)} %get-tuple-element.22), kind=kOutput, calls=%fused_computation | convolution fusion | flops 3223060480 | bytes 9175040 | tf_op jit(solution)/shard_map/dot_general | solution.py:192
  63.2 29.9 %all-to-all-done.1 = bf16[2,2,256,1024]{2,1,0,3:T(2,128)(2,1)S(1)} async-done(((bf16[2,2,256,1024]{2,1,0,3:T(2,128)(2,1)}), bf16[2,2,256,1024]{2,1,0,3:T(2,128)(2,1)S(1)}, u32[]{:S(2)}, u32[]{:S(2)}) %all-to-all-start.1) | async-done | bytes 2097184 | tf_op jit(solution)/shard_map/all_to_all | solution.py:164
  93.1 0.3 copy.52
  93.4 0.5 convert_bitcast_fusion
  93.9 0.5 copy.53
  94.4 1.8 %fusion.86 = (f32[1,256,64,32]{1,2,3,0:T(8,128)S(1)}, f32[1,256,64,32]{1,2,3,0:T(8,128)}) fusion(f32[2,256,64,32]{1,2,3,0:T(8,128)S(1)} %bitcast.59), kind=kLoop, calls=%fused_computation.99 | loop fusion | bytes 8388608 | tf_op jit(solution)/shard_map/slice | solution.py:166
  96.2 1.2 copy.56
  97.4 1.9 %copy.57 = f32[256,2048]{1,0:T(8,128)} copy(f32[256,2048]{0,1:T(8,128)S(1)} %bitcast.63) | data formatting | bytes 4194304 | tf_op jit(solution)/shard_map/squeeze | solution.py:166
  99.3 2.8 %copy.54 = f32[1,256,64,32]{1,3,2,0:T(8,128)S(1)} copy(f32[1,256,64,32]{1,2,3,0:T(8,128)} %get-tuple-element.16) | data formatting | bytes 4194304 | tf_op jit(solution)/shard_map/slice | solution.py:166
  102.1 2.1 %copy.55 = f32[256,2048]{1,0:T(8,128)} copy(f32[256,2048]{0,1:T(8,128)S(1)} %bitcast.64) | data formatting | bytes 4194304 | tf_op jit(solution)/shard_map/squeeze | solution.py:166
  104.2 0.0 copy-start.4
  104.2 0.0 copy-start.6
  104.2 4.4 %multiply_subtract_fusion = (f32[256,2048]{1,0:T(8,128)S(1)}, f32[256,2048]{1,0:T(8,128)S(1)}) fusion(f32[256,2048]{1,0:T(8,128)} %copy.57, f32[256,2048]{1,0:T(8,128)} %copy.55, f32[512,2048]{1,0:T(8,128)} %fusion), kind=kLoop, calls=%fused_computation.22 | loop fusion | flops 3145728 | bytes 12582912 | tf_op jit(solution)/shard_map/sub | solution.py:195
  108.6 0.0 copy-done.4
  108.6 0.0 copy-done.6
  108.6 3.9 %fusion.4 = f32[512,2048]{1,0:T(8,128)S(1)} fusion(f32[256,2048]{1,0:T(8,128)S(1)} %get-tuple-element.10, f32[256,2048]{1,0:T(8,128)S(1)} %get-tuple-element.9, f32[256,256]{1,0:T(8,128)S(1)} %copy-done.6, f32[256,256]{1,0:T(8,128)S(1)} %fusion.40, f32[256,256]{1,0:T(8,128)S(1)} %copy-done.4), kind=kOutput, calls=%fused_computation.4 | convolution fusion | flops 3223060480 | bytes 9175040 | tf_op jit(solution)/shard_map/dot_general | solution.py:200
  112.5 2.5 %fusion.85 = (f32[256,2048]{1,0:T(8,128)}, f32[256,2048]{1,0:T(8,128)}) fusion(f32[512,2048]{1,0:T(8,128)S(1)} %fusion.4), kind=kLoop, calls=%fused_computation.98 | loop fusion | bytes 8388608 | tf_op jit(solution)/shard_map/slice | solution.py:207
  114.9 1.9 %copy.60 = f32[256,2048]{0,1:T(8,128)S(1)} copy(f32[256,2048]{1,0:T(8,128)} %get-tuple-element.13) | data formatting | bytes 4194304 | tf_op jit(solution)/shard_map/slice | solution.py:207
  116.9 2.9 %copy.61 = f32[256,2048]{0,1:T(8,128)} copy(f32[256,2048]{1,0:T(8,128)} %get-tuple-element.14) | data formatting | bytes 4194304 | tf_op jit(solution)/shard_map/slice | solution.py:208
  119.8 0.0 copy-start
  119.8 3.1 %fusion.8 = f32[16,256,64]{1,0,2:T(8,128)S(1)} fusion(f32[256,64,32]{0,2,1:T(8,128)} %bitcast.57, f32[256,64,32]{0,2,1:T(8,128)S(1)} %bitcast.55, f32[256,32]{0,1:T(8,128)S(1)} %get-tuple-element.20, f32[256,32]{0,1:T(8,128)S(1)} %get-tuple-element.21), kind=kOutput, calls=%fused_computation.13 | convolution fusion | flops 102243328 | bytes 5308416 | tf_op jit(solution)/shard_map/ja,pca->jpc/dot_general | solution.py:28
  122.9 0.0 copy-done
  122.9 1.4 fusion.23
  124.3 0.2 convert_element_type.104
  124.5 0.2 copy.62
  124.7 26.0 %all_to_all.29 = bf16[32,128,64]{1,2,0:T(8,128)(2,1)S(1)} all-to-all(bf16[32,128,64]{1,2,0:T(8,128)(2,1)S(1)} %copy.62), channel_id=1, replica_groups=mesh['ctx'=16,'grp'=2] {'ctx','grp'}, dimensions={0} | all-to-all | bytes 1048576 | tf_op jit(solution)/shard_map/all_to_all | solution.py:216
  150.7 0.0 copy-start.2
  150.7 0.0 copy-start.8
  150.7 0.1 convert_bitcast_fusion.1
  150.9 0.1 copy.63
  150.9 1.2 copy-done.2
  152.1 0.0 copy-done.8
  152.2 0.3 fusion.27
  152.5 1.0 copy.64
Async XLA Ops:
  0.9 7.0 %collective-permute-start = (bf16[2,6144]{1,0:T(2,128)(2,1)S(1)}, bf16[2,6144]{1,0:T(2,128)(2,1)S(1)}, u32[]{:S(2)}, u32[]{:S(2)}) collective-permute-start(bf16[2,6144]{1,0:T(2,128)(2,1)S(1)} %slice.47), channel_id=1, source_target_pairs={{0,1},{1,2},{2,3},{3,4},{4,5},{5,6},{6,7},{7,8},{8,9},{9,10},{10,1... | collective-permute-start | bytes 73736 | tf_op jit(solution)/shard_map/ppermute | solution.py:14
  13.2 1.6 %copy-start.1 = (bf16[128,6144]{0,1:T(8,128)(2,1)}, bf16[128,6144]{0,1:T(8,128)(2,1)S(1)}, u32[]{:S(2)}) copy-start(bf16[128,6144]{0,1:T(8,128)(2,1)S(1)} %add_convert_fusion) | copy-start | bytes 4718596
  13.3 7.2 %copy-start.7 = (bf16[2,256,1024]{2,1,0:T(8,128)(2,1)S(1)}, bf16[2,256,1024]{2,1,0:T(8,128)(2,1)}, u32[]{:S(2)}) copy-start(bf16[2,256,1024]{2,1,0:T(8,128)(2,1)} %param.8) | copy-start | bytes 3145732
  14.8 31.9 %all-to-all-start = ((f32[128,32,64]{0,2,1:T(8,128)}), f32[128,32,64]{0,2,1:T(8,128)S(1)}, u32[]{:S(2)}, u32[]{:S(2)}) async-start(f32[128,32,64]{0,2,1:T(8,128)} %bitcast.6), calls=%async_computation | async-start | bytes 2097152 | tf_op jit(solution)/shard_map/all_to_all | solution.py:160
  47.5 45.6 %all-to-all-start.1 = ((bf16[2,2,256,1024]{2,1,0,3:T(2,128)(2,1)}), bf16[2,2,256,1024]{2,1,0,3:T(2,128)(2,1)S(1)}, u32[]{:S(2)}, u32[]{:S(2)}) async-start(bf16[2,2,256,1024]{2,1,0,3:T(2,128)(2,1)} %pad_maximum_fusion), calls=%async_computation.1 | async-start | bytes 4194304 | tf_op jit(solution)/shard_map/all_to_all | solution.py:164
  53.8 4.3 %copy-start.3 = (f32[256,256]{1,0:T(8,128)}, f32[256,256]{1,0:T(8,128)S(1)}, u32[]{:S(2)}) copy-start(f32[256,256]{1,0:T(8,128)S(1)} %get-tuple-element.22) | copy-start | bytes 786436
  53.8 4.3 %copy-start.5 = (f32[256,256]{1,0:T(8,128)}, f32[256,256]{1,0:T(8,128)S(1)}, u32[]{:S(2)}) copy-start(f32[256,256]{1,0:T(8,128)S(1)} %get-tuple-element.23) | copy-start | bytes 786436
  104.2 4.4 %copy-start.4 = (f32[256,256]{1,0:T(8,128)S(1)}, f32[256,256]{1,0:T(8,128)}, u32[]{:S(2)}) copy-start(f32[256,256]{1,0:T(8,128)} %copy-done.3) | copy-start | bytes 786436
  104.2 4.4 %copy-start.6 = (f32[256,256]{1,0:T(8,128)S(1)}, f32[256,256]{1,0:T(8,128)}, u32[]{:S(2)}) copy-start(f32[256,256]{1,0:T(8,128)} %copy-done.5) | copy-start | bytes 786436
  119.8 3.1 %copy-start = (f32[256,2048]{0,1:T(8,128)S(1)}, f32[256,2048]{0,1:T(8,128)}, u32[]{:S(2)}) copy-start(f32[256,2048]{0,1:T(8,128)} %copy.61) | copy-start | bytes 6291460
  150.7 1.4 copy-start.2
  150.7 1.4 copy-start.8

commit v2 on v1

--- a/solution.py
+++ b/solution.py
@@ -157,12 +157,22 @@
 
     outgoing = gated.reshape(row_count, group_count, block_count, width).transpose(0, 2, 1, 3)
     outgoing = outgoing.reshape(row_count, devices, width)
+    outgoing = outgoing.astype(jnp.bfloat16)
     tokens = lax.all_to_all(outgoing, everyone, split_axis=1, concat_axis=0, tiled=True)
-    tokens = tokens.reshape(block_count, block_len, width)
-
-    tokens, spectrum = lax.optimization_barrier((tokens, jnp.stack([spectrum_real, spectrum_imag])))
-    spectrum = lax.all_to_all(spectrum, "ctx", split_axis=3, concat_axis=1, tiled=True)
-    spectrum = spectrum.transpose(0, 2, 3, 1).astype(jnp.float32)
+    tokens = tokens.reshape(block_count, block_len, width).astype(jnp.float32)
+
+    local_residues, spectrum_len, half = spectrum_real.shape
+    spectrum = jnp.stack([spectrum_real, spectrum_imag])
+    spectrum = spectrum.reshape(2, local_residues, spectrum_len, block_count, width)
+    spectrum = spectrum.transpose(3, 0, 1, 2, 4)
+    share = 2 * local_residues * spectrum_len * width
+    lane = 128 if share % 128 == 0 else width
+    spectrum = spectrum.reshape(block_count, share // lane, lane)
+    tokens, spectrum = lax.optimization_barrier((tokens, spectrum))
+    spectrum = lax.all_to_all(spectrum, "ctx", split_axis=0, concat_axis=0, tiled=True)
+    spectrum = spectrum.reshape(block_count, 2, local_residues, spectrum_len, width)
+    spectrum = spectrum.transpose(1, 3, 4, 0, 2).reshape(2, spectrum_len, width, residues)
+    spectrum = spectrum.astype(jnp.float32)
     filter_real, filter_imag = spectrum[0], spectrum[1]
 
     residue = jnp.arange(residues, dtype=jnp.int32)

time: 154 us -> 164 us (1.065)
  local copies, waits for them, and re-layouts: 31.1 us -> 59.3 us
  waiting for transfers between devices: 48.4 us -> 32.5 us
  other arithmetic: 16.1 us -> 13.4 us
    all_to_all x1, waiting for transfers between devices: 18.5 us -> 3.23 us  [channel_parallel(): lax.all_to_all(outgoing, everyone, split_axis=1, concat_axis=0, tiled=True)]
    slice x3, local copies, waits for them, and re-layouts: 5.79 us -> 15.6 us  [channel_parallel(): filter_real, filter_imag = (spectrum[0], spectrum[1])]
    squeeze x2 -> x4, local copies, waits for them, and re-layouts: 3.96 us -> 10.8 us  [channel_parallel(): filter_real, filter_imag = (spectrum[0], spectrum[1])]
    reshape x1, local copies, waits for them, and re-layouts: 0.29 us -> 6.23 us  [channel_parallel(): spectrum = spectrum.reshape(block_count, share // lane, lane)]
    convert_element_type x1 -> x4, local copies, waits for them, and re-layouts: 0.49 us -> 5.68 us  [the longest x1 3.94 us: channel_parallel(): spectrum = spectrum.astype(jnp.float32)]
    another operation x1 -> x0, other arithmetic: 4.05 us -> none  [channel_parallel(): jnp.stack([spectrum_real, spectrum_imag])]
    transpose x1, local copies, waits for them, and re-layouts: 1.09 us -> 3.15 us  [channel_parallel(): spectrum = spectrum.transpose(3, 0, 1, 2, 4)]
    unnamed x21 -> x25, local copies, waits for them, and re-layouts: 6.94 us -> 6.18 us
  transfers between devices with their start and end apart: 3 -> 3, of which waited for: 2 -> 2; matrix products, arithmetic and copies ran while one was open for 14% -> 17% of each run, Pallas kernels for 0% -> 0%
where the time goes in v2:
time: 164 us; the launch traced here: 163 us
  local copies, waits for them, and re-layouts  59.3 us (36%)
  waiting for transfers between devices  32.5 us (20%)
  blocking collectives  26.2 us (16%)
  matrix products  17.8 us (11%)
  starting transfers between devices  13.6 us (8%)
  other arithmetic  13.4 us (8%)
    all_to_all x1, waiting for transfers between devices, channel_parallel(): lax.all_to_all(spectrum, 'ctx', split_axis=0, concat_axis=0, tiled=True)  29.2 us
    all_to_all x1, blocking collectives, channel_parallel(): lax.all_to_all(long_blocks, everyone, split_axis=0, concat_axis=0, tiled=...  26.2 us
    slice x3, local copies, waits for them, and re-layouts, channel_parallel(): filter_real, filter_imag = (spectrum[0], spectrum[1])  15.6 us
    squeeze x4, local copies, waits for them, and re-layouts, channel_parallel(): filter_real, filter_imag = (spectrum[0], spectrum[1])  10.8 us
    dot_general x4, matrix products, contract(): jnp.einsum(form, table, data, precision=lax.Precision.HIGHEST, preferred_...  8.75 us
    reshape x1, local copies, waits for them, and re-layouts, channel_parallel(): spectrum = spectrum.reshape(block_count, share // lane, lane)  6.23 us
    unnamed x25, local copies, waits for them, and re-layouts  6.18 us
    all_to_all x1, starting transfers between devices, channel_parallel(): lax.all_to_all(outgoing, everyone, split_axis=1, concat_axis=0, tiled=True)  5.84 us
  transfers between devices with their start and end apart: 3, of which 2 were waited for; matrix products, arithmetic and copies ran while one was open for 17% of the time, Pallas kernels for 0%

profile of v2, /device:TPU:1, one launch (start us, length us, event | category | flops | bytes accessed | tf_op | source)
XLA Modules:
  0.0 163.1 jit_solution(904199007254884408)
XLA Ops:
  0.0 0.9 slice.49
  0.9 3.9 %collective-permute-start = (bf16[2,6144]{1,0:T(2,128)(2,1)S(1)}, bf16[2,6144]{1,0:T(2,128)(2,1)S(1)}, u32[]{:S(2)}, u32[]{:S(2)}) collective-permute-start(bf16[2,6144]{1,0:T(2,128)(2,1)S(1)} %slice.49), channel_id=1, source_target_pairs={{0,1},{1,2},{2,3},{3,4},{4,5},{5,6},{6,7},{7,8},{8,9},{9,10},{10,1... | collective-permute-start | bytes 73736 | tf_op jit(solution)/shard_map/ppermute | solution.py:14
  4.9 1.1 fusion.88
  6.0 1.9 %copy.44 = bf16[128,6144]{0,1:T(8,128)(2,1)S(1)} copy(bf16[128,6144]{1,0:T(8,128)(2,1)} %param.5) | data formatting | bytes 3145728 | tf_op args[0]
  7.9 0.0 collective-permute-done
  7.9 0.9 copy.45
  8.8 4.4 %add_convert_fusion = bf16[128,6144]{0,1:T(8,128)(2,1)S(1)} fusion(bf16[128,6144]{0,1:T(8,128)(2,1)S(1)} %copy.44, bf16[2,6144]{0,1:T(8,128)(2,1)S(1)} %copy.45, f32[6144]{0:T(1024)S(1)} %bitcast.69, f32[6144]{0:T(1024)S(1)} %bitcast.70, f32[6144]{0:T(1024)S(1)} %bitcast.68), kind=kLoop, calls=%fused_computation.10 | loop fusion | flops 11796480 | bytes 3244032 | tf_op jit(solution)/shard_map/convert_element_type | solution.py:132
  13.2 0.0 copy-start.1
  13.2 1.2 copy-done.1
  14.4 0.1 fusion.32
  14.5 0.0 copy-start.9
  14.5 0.8 copy.47
  15.4 5.8 %all-to-all-start = ((bf16[128,32,64]{0,2,1:T(8,128)(2,1)}), bf16[128,32,64]{0,2,1:T(8,128)(2,1)}, u32[]{:S(2)}, u32[]{:S(2)}) async-start(bf16[128,32,64]{0,2,1:T(8,128)(2,1)} %bitcast.6), calls=%async_computation | async-start | bytes 1048576 | tf_op jit(solution)/shard_map/all_to_all | solution.py:161
  21.2 0.0 copy-done.8
  21.2 0.5 copy.50
  21.8 0.0 copy-done.9
  21.8 1.3 copy.49
  23.1 1.4 maximum_bitcast_fusion
  24.5 3.1 %copy.51 = bf16[16,2,2,256,64]{4,3,2,1,0:T(8,128)(2,1)} copy(bf16[16,2,2,256,64]{3,4,0,2,1:T(8,128)(2,1)S(1)} %maximum_bitcast_fusion) | data formatting | bytes 4194304 | tf_op jit(solution)/shard_map/transpose | solution.py:167
  27.7 6.2 %reshape.94 = bf16[16,512,128]{2,1,0:T(8,128)(2,1)} reshape(bf16[16,2,2,256,64]{4,3,2,1,0:T(8,128)(2,1)} %copy.51) | data formatting | bytes 4194304 | tf_op jit(solution)/shard_map/reshape | solution.py:170
  33.9 3.2 %all-to-all-done = bf16[128,32,64]{0,2,1:T(8,128)(2,1)} async-done(((bf16[128,32,64]{0,2,1:T(8,128)(2,1)}), bf16[128,32,64]{0,2,1:T(8,128)(2,1)}, u32[]{:S(2)}, u32[]{:S(2)}) %all-to-all-start) | async-done | bytes 524320 | tf_op jit(solution)/shard_map/all_to_all | solution.py:161
  37.1 1.1 convert_bitcast_fusion.1
  38.3 0.6 copy.48
  38.9 0.3 reshape.102
  39.2 3.8 %all-to-all-start.1 = ((bf16[16,512,128]{2,1,0:T(8,128)(2,1)}), bf16[16,512,128]{2,1,0:T(8,128)(2,1)S(1)}, u32[]{:S(2)}, u32[]{:S(2)}) async-start(bf16[16,512,128]{2,1,0:T(8,128)(2,1)} %reshape.94), calls=%async_computation.1 | async-start | bytes 4194304 | tf_op jit(solution)/shard_map/all_to_all | solution.py:172
  43.0 0.1 fusion.48
  43.2 1.0 fusion.41
  44.1 1.0 fusion.39
  45.2 0.0 copy-start.4
  45.2 0.0 copy-start.6
  45.2 1.9 %fusion.54 = f32[256,64,32]{0,2,1:T(8,128)S(1)} fusion(f32[16,256,64]{1,0,2:T(8,128)S(1)} %reshape.102), kind=kOutput, calls=%fused_computation.71 | convolution fusion | flops 100670464 | bytes 3145728 | tf_op jit(solution)/shard_map/jpc,ja->pca/dot_general | solution.py:28
  47.1 2.3 %multiply_add_fusion.1 = (f32[256,64,32]{0,2,1:T(8,128)S(1)}, f32[256,64,32]{0,2,1:T(8,128)S(1)}) fusion(f32[256,64,32]{0,2,1:T(8,128)S(1)} %fusion.54, f32[256,32]{0,1:T(8,128)S(1)} %get-tuple-element.20, f32[256,32]{0,1:T(8,128)S(1)} %get-tuple-element.21, f32[16,256,64]{1,0,2:T(8,128)S(1)} %reshape.102), kind=kOutput, calls=%fused_computation.23 | convolution fusion | flops 104340480 | bytes 7405568 | tf_op jit(solution)/shard_map/jpc,ja->pca/dot_general | solution.py:28
  49.4 0.0 copy-done.4
  49.5 0.0 copy-done.6
  49.5 5.2 %fusion = f32[512,2048]{1,0:T(8,128)} fusion(f32[256,2048]{0,1:T(8,128)S(1)} %bitcast.63, f32[256,2048]{0,1:T(8,128)S(1)} %bitcast.62, f32[256,256]{1,0:T(8,128)S(1)} %get-tuple-element.23, f32[256,256]{1,0:T(8,128)S(1)} %fusion.41, f32[256,256]{1,0:T(8,128)S(1)} %get-tuple-element.22), kind=kOutput, calls=%fused_computation | convolution fusion | flops 3223060480 | bytes 9175040 | tf_op jit(solution)/shard_map/dot_general | solution.py:202
  54.7 29.2 %all-to-all-done.1 = bf16[16,512,128]{2,1,0:T(8,128)(2,1)S(1)} async-done(((bf16[16,512,128]{2,1,0:T(8,128)(2,1)}), bf16[16,512,128]{2,1,0:T(8,128)(2,1)S(1)}, u32[]{:S(2)}, u32[]{:S(2)}) %all-to-all-start.1) | async-done | bytes 2097184 | tf_op jit(solution)/shard_map/all_to_all | solution.py:172
  83.9 3.9 %reshape.105 = f32[16,2,2,256,64]{4,3,2,1,0:T(8,128)} reshape(bf16[16,512,128]{2,1,0:T(8,128)(2,1)S(1)} %all-to-all-done.1) | data formatting | bytes 6291456 | tf_op jit(solution)/shard_map/convert_element_type | solution.py:175
  87.8 7.7 %fusion.86 = (f32[1,256,64,16,2]{2,1,4,0,3:T(8,128)}, f32[1,256,64,16,2]{2,1,4,0,3:T(8,128)}) fusion(f32[2,256,64,16,2]{2,1,4,0,3:T(8,128)} %bitcast.57), kind=kLoop, calls=%fused_computation.99 | loop fusion | bytes 8388608 | tf_op jit(solution)/shard_map/slice | solution.py:176
  95.5 4.0 %copy.54 = f32[1,256,64,16,2]{1,4,3,2,0:T(2,128)S(1)} copy(f32[1,256,64,16,2]{2,1,4,0,3:T(8,128)} %get-tuple-element.11) | data formatting | bytes 4194304 | tf_op jit(solution)/shard_map/slice | solution.py:176
  99.5 2.4 %squeeze.7 = f32[256,2048]{0,1:T(8,128)} reshape(f32[1,256,64,16,2]{1,4,3,2,0:T(2,128)S(1)} %copy.54) | data formatting | bytes 4194304 | tf_op jit(solution)/shard_map/squeeze | solution.py:176
  101.9 2.9 %copy.55 = f32[256,2048]{1,0:T(8,128)} copy(f32[256,2048]{0,1:T(8,128)} %squeeze.7) | data formatting | bytes 4194304 | tf_op jit(solution)/shard_map/squeeze | solution.py:176
  104.8 4.0 %copy.52 = f32[1,256,64,16,2]{1,4,3,2,0:T(2,128)S(1)} copy(f32[1,256,64,16,2]{2,1,4,0,3:T(8,128)} %get-tuple-element.12) | data formatting | bytes 4194304 | tf_op jit(solution)/shard_map/slice | solution.py:176
  108.8 2.5 %squeeze.6 = f32[256,2048]{0,1:T(8,128)} reshape(f32[1,256,64,16,2]{1,4,3,2,0:T(2,128)S(1)} %copy.52) | data formatting | bytes 4194304 | tf_op jit(solution)/shard_map/squeeze | solution.py:176
  111.3 3.0 %copy.53 = f32[256,2048]{1,0:T(8,128)} copy(f32[256,2048]{0,1:T(8,128)} %squeeze.6) | data formatting | bytes 4194304 | tf_op jit(solution)/shard_map/squeeze | solution.py:176
  114.3 0.0 copy-done.3
  114.3 3.8 %multiply_subtract_fusion = (f32[256,2048]{1,0:T(8,128)S(1)}, f32[256,2048]{1,0:T(8,128)S(1)}) fusion(f32[256,2048]{1,0:T(8,128)S(1)} %copy-done.3, f32[256,2048]{1,0:T(8,128)} %copy.53, f32[512,2048]{1,0:T(8,128)} %fusion), kind=kLoop, calls=%fused_computation.21 | loop fusion | flops 3145728 | bytes 12582912 | tf_op jit(solution)/shard_map/sub | solution.py:205
  118.1 0.0 copy-done.5
  118.1 0.0 copy-done.7
  118.1 3.9 %fusion.4 = f32[512,2048]{1,0:T(8,128)S(1)} fusion(f32[256,2048]{1,0:T(8,128)S(1)} %get-tuple-element.10, f32[256,2048]{1,0:T(8,128)S(1)} %get-tuple-element.9, f32[256,256]{1,0:T(8,128)S(1)} %copy-done.7, f32[256,256]{1,0:T(8,128)S(1)} %fusion.41, f32[256,256]{1,0:T(8,128)S(1)} %copy-done.5), kind=kOutput, calls=%fused_computation.4 | convolution fusion | flops 3223060480 | bytes 9175040 | tf_op jit(solution)/shard_map/dot_general | solution.py:210
  122.0 2.4 %fusion.87 = (f32[256,2048]{1,0:T(8,128)}, f32[256,2048]{1,0:T(8,128)}) fusion(f32[512,2048]{1,0:T(8,128)S(1)} %fusion.4), kind=kLoop, calls=%fused_computation.100 | loop fusion | bytes 8388608 | tf_op jit(solution)/shard_map/slice | solution.py:217
  124.4 1.9 %copy.59 = f32[256,2048]{0,1:T(8,128)S(1)} copy(f32[256,2048]{1,0:T(8,128)} %get-tuple-element.16) | data formatting | bytes 4194304 | tf_op jit(solution)/shard_map/slice | solution.py:218
  126.4 2.9 %copy.58 = f32[256,2048]{0,1:T(8,128)} copy(f32[256,2048]{1,0:T(8,128)} %get-tuple-element.15) | data formatting | bytes 4194304 | tf_op jit(solution)/shard_map/slice | solution.py:217
  129.2 3.1 %fusion.8 = f32[16,256,64]{1,0,2:T(8,128)S(1)} fusion(f32[256,64,32]{0,2,1:T(8,128)S(1)} %bitcast.58, f32[256,64,32]{0,2,1:T(8,128)} %bitcast.60, f32[256,32]{0,1:T(8,128)S(1)} %get-tuple-element.20, f32[256,32]{0,1:T(8,128)S(1)} %get-tuple-element.21), kind=kOutput, calls=%fused_computation.12 | convolution fusion | flops 102243328 | bytes 5308416 | tf_op jit(solution)/shard_map/ja,pca->jpc/dot_general | solution.py:28
  132.3 0.0 copy-done
  132.4 1.4 fusion.23
  133.8 0.2 convert_element_type.129
  134.0 0.2 copy.60
  134.2 26.2 %all_to_all.19 = bf16[32,128,64]{1,2,0:T(8,128)(2,1)S(1)} all-to-all(bf16[32,128,64]{1,2,0:T(8,128)(2,1)S(1)} %copy.60), channel_id=1, replica_groups=mesh['ctx'=16,'grp'=2] {'ctx','grp'}, dimensions={0} | all-to-all | bytes 1048576 | tf_op jit(solution)/shard_map/all_to_all | solution.py:226
  160.4 0.1 convert_bitcast_fusion
  160.5 0.1 copy.61
  160.6 1.2 copy-done.2
  161.8 0.0 copy-done.10
  161.8 0.3 fusion.27
  162.1 1.0 copy.62
  (7 shorter events, 0.0 us)
Async XLA Ops:
  0.9 7.0 %collective-permute-start = (bf16[2,6144]{1,0:T(2,128)(2,1)S(1)}, bf16[2,6144]{1,0:T(2,128)(2,1)S(1)}, u32[]{:S(2)}, u32[]{:S(2)}) collective-permute-start(bf16[2,6144]{1,0:T(2,128)(2,1)S(1)} %slice.49), channel_id=1, source_target_pairs={{0,1},{1,2},{2,3},{3,4},{4,5},{5,6},{6,7},{7,8},{8,9},{9,10},{10,1... | collective-permute-start | bytes 73736 | tf_op jit(solution)/shard_map/ppermute | solution.py:14
  13.2 1.2 copy-start.1
  14.4 6.8 %copy-start.8 = (bf16[2,256,1024]{2,1,0:T(8,128)(2,1)S(1)}, bf16[2,256,1024]{2,1,0:T(8,128)(2,1)}, u32[]{:S(2)}) copy-start(bf16[2,256,1024]{2,1,0:T(8,128)(2,1)} %param.9) | copy-start | bytes 3145732
  14.5 7.2 %copy-start.9 = (bf16[2,256,1024]{2,1,0:T(8,128)(2,1)S(1)}, bf16[2,256,1024]{2,1,0:T(8,128)(2,1)}, u32[]{:S(2)}) copy-start(bf16[2,256,1024]{2,1,0:T(8,128)(2,1)} %param.8) | copy-start | bytes 3145732
  15.4 21.7 %all-to-all-start = ((bf16[128,32,64]{0,2,1:T(8,128)(2,1)}), bf16[128,32,64]{0,2,1:T(8,128)(2,1)}, u32[]{:S(2)}, u32[]{:S(2)}) async-start(bf16[128,32,64]{0,2,1:T(8,128)(2,1)} %bitcast.6), calls=%async_computation | async-start | bytes 1048576 | tf_op jit(solution)/shard_map/all_to_all | solution.py:161
  39.2 44.7 %all-to-all-start.1 = ((bf16[16,512,128]{2,1,0:T(8,128)(2,1)}), bf16[16,512,128]{2,1,0:T(8,128)(2,1)S(1)}, u32[]{:S(2)}, u32[]{:S(2)}) async-start(bf16[16,512,128]{2,1,0:T(8,128)(2,1)} %reshape.94), calls=%async_computation.1 | async-start | bytes 4194304 | tf_op jit(solution)/shard_map/all_to_all | solution.py:172
  45.2 4.3 %copy-start.4 = (f32[256,256]{1,0:T(8,128)}, f32[256,256]{1,0:T(8,128)S(1)}, u32[]{:S(2)}) copy-start(f32[256,256]{1,0:T(8,128)S(1)} %get-tuple-element.22) | copy-start | bytes 786436
  45.2 4.3 %copy-start.6 = (f32[256,256]{1,0:T(8,128)}, f32[256,256]{1,0:T(8,128)S(1)}, u32[]{:S(2)}) copy-start(f32[256,256]{1,0:T(8,128)S(1)} %get-tuple-element.23) | copy-start | bytes 786436
  111.3 3.0 %copy-start.3 = (f32[256,2048]{1,0:T(8,128)S(1)}, f32[256,2048]{1,0:T(8,128)}, u32[]{:S(2)}) copy-start(f32[256,2048]{1,0:T(8,128)} %copy.55) | copy-start | bytes 6291460
  114.3 3.8 %copy-start.5 = (f32[256,256]{1,0:T(8,128)S(1)}, f32[256,256]{1,0:T(8,128)}, u32[]{:S(2)}) copy-start(f32[256,256]{1,0:T(8,128)} %copy-done.4) | copy-start | bytes 786436
  114.3 3.8 %copy-start.7 = (f32[256,256]{1,0:T(8,128)S(1)}, f32[256,256]{1,0:T(8,128)}, u32[]{:S(2)}) copy-start(f32[256,256]{1,0:T(8,128)} %copy-done.6) | copy-start | bytes 786436
  129.2 3.1 %copy-start = (f32[256,2048]{0,1:T(8,128)S(1)}, f32[256,2048]{0,1:T(8,128)}, u32[]{:S(2)}) copy-start(f32[256,2048]{0,1:T(8,128)} %copy.58) | copy-start | bytes 6291460
  160.4 1.4 copy-start.2
  160.4 1.4 copy-start.10
